TPU v7x, 32 devices: a whole 2x2x4 slice. The times are simulated.
32 devices in a mesh: grp: 2 (over y), seq: 4 (over z), head: 2 (over x), sub: 2 (over core).
Axes of the slice: x: 2, y: 2, z: 4, core: 2. Of those that a mesh axis runs over, the one named last changes fastest.
Arguments:
- queries: bfloat16 [4096, 64, 128], P(('grp', 'seq'), ('head', 'sub')), parts along dimension 0, may hold values from -6 to 6
- key_rows: bfloat16 [4096, 64, 128], P(('grp', 'seq'), ('head', 'sub')), parts along dimension 0, may hold values from -6 to 6
- value_rows: bfloat16 [4096, 64, 128], P(('grp', 'seq'), ('head', 'sub')), parts along dimension 0, may hold values from -6 to 6
- out_adjoint: bfloat16 [4096, 64, 128], P(('grp', 'seq'), ('head', 'sub')), parts along dimension 0, may hold values from -6 to 6
Outputs:
- attended: bfloat16 [4096, 64, 128], P(('grp', 'seq'), ('head', 'sub')), parts along dimension 0
- query_grad: bfloat16 [4096, 64, 128], P(('grp', 'seq', 'head', 'sub')), parts along dimension 0
- key_grad: bfloat16 [4096, 64, 128], P(('grp', 'seq', 'head', 'sub')), parts along dimension 0
- value_grad: bfloat16 [4096, 64, 128], P(('grp', 'seq', 'head', 'sub')), parts along dimension 0
There are 2 independent parts, one for each index of `grp`. A program takes and returns all parts, laid end to end along the dimension named above; each array names one. Nothing has to cross between parts.
All inputs are finite; a program needn't handle non-finite values.
Results may differ from a plain program's by a relative error of at most 0.0058.
Values may be sent and summed in bfloat16 or wider, within the bound.
No kernel may reach another device: no remote copies, remote signals or barrier semaphores. Data moves between devices by JAX's collectives and lax.ppermute only.
A program may use at most 128 MiB of HBM per device.

v0:
```python
import jax
import jax.numpy as jnp
from jax import lax
from jax.sharding import PartitionSpec as P

SPAN = 64


def prefix(part, axis, combine, identity, reverse):
    count = lax.axis_size(axis)
    place = lax.axis_index(axis)
    ahead = count - 1 - place if reverse else place
    gathered = lax.all_gather(part, axis)
    state = jnp.zeros_like(part) + jnp.asarray(identity, part.dtype)

    def one(turn, state):
        source = count - 1 - turn if reverse else turn
        return combine(state, lax.dynamic_index_in_dim(gathered, source, 0, False))

    return lax.fori_loop(0, ahead, one, state)


def add_states(earlier, later):
    return earlier + later


def per_device(queries, key_rows, value_rows, out_adjoint):
    tok_dev, heads_dev, head_dim = queries.shape
    span = SPAN
    blocks = tok_dev // span
    offset = lax.axis_index("seq") * tok_dev
    position = offset + jnp.arange(tok_dev, dtype=jnp.int32)
    factor = lax.rsqrt(jnp.float32(head_dim) * (position + 1).astype(jnp.float32))
    scaled = (queries.astype(jnp.float32) * factor[:, None, None]).astype(jnp.bfloat16)
    qsc = scaled.reshape(blocks, span, heads_dev, head_dim)
    kch = key_rows.reshape(blocks, span, heads_dev, head_dim)
    vch = value_rows.reshape(blocks, span, heads_dev, head_dim)
    dch = out_adjoint.reshape(blocks, span, heads_dev, head_dim)
    kv_block = jnp.einsum("nchd,nche->nhde", kch, vch, preferred_element_type=jnp.float32)
    adj_block = jnp.einsum("nche,nchd->nhed", dch, qsc, preferred_element_type=jnp.float32)
    kv_total = jnp.sum(kv_block, 0)
    adj_total = jnp.sum(adj_block, 0)
    zeros = jnp.zeros_like(kv_total)
    before = prefix(kv_total, "seq", add_states, zeros, False)
    after = prefix(adj_total, "seq", add_states, zeros, True)
    state = before[None] + jnp.cumsum(kv_block, 0) - kv_block
    suffix = after[None] + jnp.cumsum(adj_block[::-1], 0)[::-1] - adj_block
    state_low = state.astype(jnp.bfloat16)
    suffix_low = suffix.astype(jnp.bfloat16)
    row = jnp.arange(span, dtype=jnp.int32)
    causal = (row[:, None] >= row[None, :])[None, None]
    scores = jnp.where(
        causal, jnp.einsum("nchd,nshd->nhcs", qsc, kch, preferred_element_type=jnp.float32), 0.0
    ).astype(jnp.bfloat16)
    attended = jnp.einsum(
        "nchd,nhde->nche", qsc, state_low, preferred_element_type=jnp.float32
    ) + jnp.einsum("nhcs,nshe->nche", scores, vch, preferred_element_type=jnp.float32)
    adj_scores = jnp.where(
        causal, jnp.einsum("nche,nshe->nhcs", dch, vch, preferred_element_type=jnp.float32), 0.0
    ).astype(jnp.bfloat16)
    query_grad = (
        jnp.einsum("nche,nhde->nchd", dch, state_low, preferred_element_type=jnp.float32)
        + jnp.einsum("nhcs,nshd->nchd", adj_scores, kch, preferred_element_type=jnp.float32)
    ) * factor.reshape(blocks, span, 1, 1)
    key_grad = jnp.einsum(
        "nshe,nhed->nshd", vch, suffix_low, preferred_element_type=jnp.float32
    ) + jnp.einsum("nhcs,nchd->nshd", adj_scores, qsc, preferred_element_type=jnp.float32)
    value_grad = jnp.einsum(
        "nshd,nhed->nshe", kch, suffix_low, preferred_element_type=jnp.float32
    ) + jnp.einsum("nhcs,nche->nshe", scores, dch, preferred_element_type=jnp.float32)
    shape = (tok_dev, heads_dev, head_dim)
    attended = attended.reshape(shape).astype(jnp.bfloat16)
    query_grad = query_grad.reshape(shape).astype(jnp.bfloat16)
    key_grad = key_grad.reshape(shape).astype(jnp.bfloat16)
    value_grad = value_grad.reshape(shape).astype(jnp.bfloat16)
    query_out, key_out, value_out = (
        lax.all_to_all(query_grad, ("head", "sub"), split_axis=0, concat_axis=1, tiled=True),
        lax.all_to_all(key_grad, ("head", "sub"), split_axis=0, concat_axis=1, tiled=True),
        lax.all_to_all(value_grad, ("head", "sub"), split_axis=0, concat_axis=1, tiled=True),
    )
    return (attended, query_out, key_out, value_out)


def solution(mesh):
    in_specs = (
        P(("grp", "seq"), ("head", "sub"), None),
        P(("grp", "seq"), ("head", "sub"), None),
        P(("grp", "seq"), ("head", "sub"), None),
        P(("grp", "seq"), ("head", "sub"), None),
    )
    out_specs = (
        P(("grp", "seq"), ("head", "sub"), None),
        P(("grp", "seq", "head", "sub"), None, None),
        P(("grp", "seq", "head", "sub"), None, None),
        P(("grp", "seq", "head", "sub"), None, None),
    )
    return jax.shard_map(
        per_device, mesh=mesh, in_specs=in_specs, out_specs=out_specs, check_vma=False
    )
```

profile of v0, /device:TPU:0, one launch (start us, length us, event | category | flops | bytes accessed | tf_op | source)
XLA Modules:
  0.0 252.0 jit_solution(12167041707173029540)
XLA Ops:
  7.3 2.9 %multiply_convert_fusion = bf16[512,16,128]{2,1,0:T(8,128)(2,1)S(1)} fusion(bf16[512,16,128]{2,1,0:T(8,128)(2,1)} %param.8, f32[512]{0:T(512)S(1)} %multiply_rsqrt_fusion.1), kind=kLoop, calls=%fused_computation.14 | loop fusion | flops 3145728 | bytes 4196352 | tf_op jit(solution)/shard_map/convert_element_type | solution.py:34
  10.2 5.0 %fusion.27 = (f32[16,128,128]{1,2,0:T(8,128)S(1)}, f32[8,16,128,128]{2,3,1,0:T(8,128)}) fusion(bf16[8,64,16,128]{3,2,1,0:T(8,128)(2,1)S(1)} %bitcast.73, bf16[8,64,16,128]{3,2,1,0:T(8,128)(2,1)S(1)} %bitcast.68), kind=kOutput, calls=%fused_computation.42 | convolution fusion | flops 270270464 | bytes 13631488 | tf_op jit(solution)/shard_map/nche,nchd->nhed/dot_general | solution.py:40
  16.5 7.6 %fusion.26 = (f32[16,128,128]{2,1,0:T(8,128)}, f32[8,16,128,128]{3,2,1,0:T(8,128)}) fusion(bf16[8,64,16,128]{3,2,1,0:T(8,128)(2,1)S(1)} %bitcast.64, bf16[8,64,16,128]{3,2,1,0:T(8,128)(2,1)} %bitcast.76), kind=kOutput, calls=%fused_computation.41 | convolution fusion | flops 270270464 | bytes 13631488 | tf_op jit(solution)/shard_map/nchd,nche->nhde/dot_general | solution.py:39
  24.1 8.3 %rev.6 = f32[8,16,128,128]{2,3,1,0:T(8,128)} reverse(f32[8,16,128,128]{2,3,1,0:T(8,128)} %get-tuple-element.104), dimensions={0} | reverse | bytes 16777216 | tf_op jit(solution)/shard_map/rev | solution.py:47
  32.5 4.3 %select_convert_fusion = bf16[8,16,64,64]{3,2,1,0:T(8,128)(2,1)} fusion(pred[64,64]{1,0:T(8,128)(4,1)S(1)} %iota_compare_fusion, bf16[8,64,16,128]{3,2,1,0:T(8,128)(2,1)} %bitcast.72, bf16[8,64,16,128]{3,2,1,0:T(8,128)(2,1)S(1)} %bitcast.66), kind=kOutput, calls=%fused_computation.12 | convolution fusion | flops 135266304 | bytes 5246976 | tf_op jit(solution)/shard_map/nche,nshe->nhcs/dot_general | solution.py:59
  39.4 2.8 %fusion.5 = f32[8,16,64,128]{3,2,1,0:T(8,128)} fusion(bf16[8,16,64,64]{3,2,1,0:T(8,128)(2,1)S(1)} %select_convert_fusion.1, bf16[8,64,16,128]{3,2,1,0:T(8,128)(2,1)S(1)} %bitcast.74), kind=kOutput, calls=%fused_computation.17 | convolution fusion | flops 134217728 | bytes 7340032 | tf_op jit(solution)/shard_map/nhcs,nche->nshe/dot_general | solution.py:70
  42.2 8.3 %fusion.28 = f32[8,16,128,128]{2,3,1,0:T(8,128)} fusion(f32[8,16,128,128]{2,3,1,0:T(8,128)} %rev.6), kind=kOutput, calls=%fused_computation.43 | output fusion | flops 14680064 | bytes 16777216 | tf_op jit(solution)/shard_map/jit(cumsum)/reduce_window_sum | solution.py:47
  50.5 49.6 %all-gather.7.cloned.1.call-done = f32[64,128,128]{2,1,0:T(8,128)} async-done(((f32[16,128,128]{2,1,0:T(8,128)}), f32[64,128,128]{2,1,0:T(8,128)}) %all-gather.7.cloned.1.call-update) | async-done | bytes 4194320 | tf_op jit(solution)/shard_map/all_gather | solution.py:13
  100.2 4.7 %while.23 = (s32[]{:T(128)}, f32[16,128,128]{2,1,0:T(8,128)S(1)}, s32[]{:T(128)}, f32[4,16,128,128]{3,2,1,0:T(8,128)}, s32[]{:T(128)}, /*index=5*/s32[]{:T(128)}, s32[]{:T(128)}, s32[]{:T(128)}) while((s32[]{:T(128)}, f32[16,128,128]{2,1,0:T(8,128)S(1)}, s32[]{:T(128)}, f32[4,16,128,128]{3,2,1,0:T(8,128)}, s32[]{:T(128)}, ...), condition=%wide.region_6.7_spmd, body=%wide.region_5.6_spmd.sunk | while | flops 262150 | bytes 3145863 | solution.py:20
  106.2 11.1 %subtract_convert_fusion = bf16[8,16,128,128]{2,3,1,0:T(8,128)(2,1)} fusion(f32[8,16,128,128]{2,3,1,0:T(8,128)} %get-tuple-element.104, f32[8,16,128,128]{2,3,1,0:T(8,128)} %fusion.28, f32[16,128,128]{1,2,0:T(8,128)} %copy.98), kind=kLoop, calls=%fused_computation.2 | loop fusion | flops 6291456 | bytes 22020096 | tf_op jit(solution)/shard_map/convert_element_type | solution.py:49
  117.3 5.3 %fusion.15 = f32[8,16,128,64]{2,3,1,0:T(8,128)S(1)} fusion(bf16[8,16,128,128]{2,3,1,0:T(8,128)(2,1)} %subtract_convert_fusion, bf16[8,64,16,128]{3,2,1,0:T(8,128)(2,1)S(1)} %bitcast.65), kind=kOutput, calls=%fused_computation.27 | convolution fusion | flops 268435456 | bytes 10485760 | tf_op jit(solution)/shard_map/nshe,nhed->nshd/dot_general | solution.py:65
  126.6 4.5 %all-to-all-start.1 = ((bf16[512,16,128]{2,1,0:T(8,128)(2,1)}), bf16[512,16,128]{2,1,0:T(8,128)(2,1)}, u32[]{:S(2)}, u32[]{:S(2)}) async-start(bf16[512,16,128]{2,1,0:T(8,128)(2,1)} %bitcast.81), calls=%async_computation.1 | async-start | bytes 4194304 | tf_op jit(solution)/shard_map/all_to_all | solution.py:78
  131.1 5.4 %fusion = bf16[8,64,16,128]{3,1,2,0:T(8,128)(2,1)S(1)} fusion(f32[8,16,64,128]{3,2,1,0:T(8,128)} %fusion.5, bf16[8,16,128,128]{2,3,1,0:T(8,128)(2,1)} %subtract_convert_fusion, bf16[8,64,16,128]{3,2,1,0:T(8,128)(2,1)} %bitcast.77), kind=kOutput, calls=%fused_computation.5 | convolution fusion | flops 270532608 | bytes 12582912 | tf_op jit(solution)/shard_map/nshd,nhed->nshe/dot_general | solution.py:68
  136.5 2.8 %copy.109 = bf16[8,64,16,128]{3,2,1,0:T(8,128)(2,1)} copy(bf16[8,64,16,128]{3,1,2,0:T(8,128)(2,1)S(1)} %fusion) | data formatting | bytes 4194304 | tf_op jit(solution)/shard_map/convert_element_type | solution.py:75
  139.3 41.7 %all-gather.5.cloned.1.call-done = f32[64,128,128]{2,1,0:T(8,128)} async-done(((f32[16,128,128]{2,1,0:T(8,128)}), f32[64,128,128]{2,1,0:T(8,128)}) %all-gather.5.cloned.1.call-update) | async-done | bytes 4194320 | tf_op jit(solution)/shard_map/all_gather | solution.py:13
  181.1 4.7 %all-to-all-start.2 = ((bf16[512,16,128]{2,1,0:T(8,128)(2,1)}), bf16[512,16,128]{2,1,0:T(8,128)(2,1)}, u32[]{:S(2)}, u32[]{:S(2)}) async-start(bf16[512,16,128]{2,1,0:T(8,128)(2,1)} %bitcast.80), calls=%async_computation.2 | async-start | bytes 4194304 | tf_op jit(solution)/shard_map/all_to_all | solution.py:79
  185.9 7.0 %subtract_convert_fusion.1 = bf16[8,16,128,128]{3,2,1,0:T(8,128)(2,1)S(1)} fusion(f32[8,16,128,128]{3,2,1,0:T(8,128)} %get-tuple-element.102, f32[16,128,128]{2,1,0:T(8,128)S(1)} %get-tuple-element.83), kind=kOutput, calls=%fused_computation.3 | output fusion | flops 20971520 | bytes 13631488 | tf_op jit(solution)/shard_map/jit(cumsum)/reduce_window_sum | solution.py:46
  192.9 3.0 %fusion.9 = f32[8,16,128,64]{2,3,1,0:T(8,128)S(1)} fusion(bf16[8,16,128,128]{3,2,1,0:T(8,128)(2,1)S(1)} %subtract_convert_fusion.1, bf16[8,64,16,128]{3,2,1,0:T(8,128)(2,1)S(1)} %bitcast.75), kind=kOutput, calls=%fused_computation.21 | convolution fusion | flops 268435456 | bytes 10485760 | tf_op jit(solution)/shard_map/nche,nhde->nchd/dot_general | solution.py:62
  200.4 11.0 %all-to-all-done.2 = bf16[512,16,128]{2,1,0:T(8,128)(2,1)} async-done(((bf16[512,16,128]{2,1,0:T(8,128)(2,1)}), bf16[512,16,128]{2,1,0:T(8,128)(2,1)}, u32[]{:S(2)}, u32[]{:S(2)}) %all-to-all-start.2) | async-done | bytes 2097184 | tf_op jit(solution)/shard_map/all_to_all | solution.py:79
  211.4 4.4 %all-to-all-start = ((bf16[512,16,128]{2,1,0:T(8,128)(2,1)}), bf16[512,16,128]{2,1,0:T(8,128)(2,1)}, u32[]{:S(2)}, u32[]{:S(2)}) async-start(bf16[512,16,128]{2,1,0:T(8,128)(2,1)} %bitcast.82), calls=%async_computation | async-start | bytes 4194304 | tf_op jit(solution)/shard_map/all_to_all | solution.py:77
  223.3 3.6 %copy.104 = bf16[128,4,16,128]{3,2,1,0:T(8,128)(2,1)} copy(bf16[128,4,16,128]{3,2,0,1:T(8,128)(2,1)} %bitcast.21) | data formatting | bytes 4194304 | tf_op jit(solution)/shard_map/all_to_all | solution.py:78
  226.9 3.6 %copy.110 = bf16[128,4,16,128]{3,2,1,0:T(8,128)(2,1)} copy(bf16[128,4,16,128]{3,2,0,1:T(8,128)(2,1)} %bitcast.27) | data formatting | bytes 4194304 | tf_op jit(solution)/shard_map/all_to_all | solution.py:79
  230.5 11.1 %all-to-all-done = bf16[512,16,128]{2,1,0:T(8,128)(2,1)} async-done(((bf16[512,16,128]{2,1,0:T(8,128)(2,1)}), bf16[512,16,128]{2,1,0:T(8,128)(2,1)}, u32[]{:S(2)}, u32[]{:S(2)}) %all-to-all-start) | async-done | bytes 2097184 | tf_op jit(solution)/shard_map/all_to_all | solution.py:77
  241.6 3.6 %copy.94 = bf16[128,4,16,128]{3,2,1,0:T(8,128)(2,1)} copy(bf16[128,4,16,128]{3,2,0,1:T(8,128)(2,1)} %bitcast.14) | data formatting | bytes 4194304 | tf_op jit(solution)/shard_map/all_to_all | solution.py:77
  (54 shorter events, 25.9 us)
Async XLA Ops:
  7.2 9.4 %copy-start = (bf16[512,16,128]{2,1,0:T(8,128)(2,1)S(1)}, bf16[512,16,128]{2,1,0:T(8,128)(2,1)}, u32[]{:S(2)}) copy-start(bf16[512,16,128]{2,1,0:T(8,128)(2,1)} %param.10) | copy-start | bytes 6291460
  7.2 92.9 %all-gather.7.cloned.1.call-start = ((), (), s32[]{:S(2)}) async-start(), calls=%async_computation.4 | async-start | bytes 5242880 | tf_op jit(solution)/shard_map/all_gather | solution.py:13
  7.2 2.9 %copy-start.7 = (bf16[512,16,128]{2,1,0:T(8,128)(2,1)S(1)}, bf16[512,16,128]{2,1,0:T(8,128)(2,1)}, u32[]{:S(2)}) copy-start(bf16[512,16,128]{2,1,0:T(8,128)(2,1)} %param.11) | copy-start | bytes 6291460
  10.1 5.0 %copy-start.3 = (bf16[512,16,128]{2,1,0:T(8,128)(2,1)}, bf16[512,16,128]{2,1,0:T(8,128)(2,1)S(1)}, u32[]{:S(2)}) copy-start(bf16[512,16,128]{2,1,0:T(8,128)(2,1)S(1)} %multiply_convert_fusion) | copy-start | bytes 6291460
  16.5 164.5 %all-gather.5.cloned.1.call-start = ((), (), s32[]{:S(2)}) async-start(), calls=%async_computation.3 | async-start | bytes 5242880 | tf_op jit(solution)/shard_map/all_gather | solution.py:13
  32.5 4.3 %copy-start.4 = (bf16[512,16,128]{2,1,0:T(8,128)(2,1)S(1)}, bf16[512,16,128]{2,1,0:T(8,128)(2,1)}, u32[]{:S(2)}) copy-start(bf16[512,16,128]{2,1,0:T(8,128)(2,1)} %copy-done.3) | copy-start | bytes 6291460
  32.5 4.3 %copy-start.10 = (bf16[512,16,128]{2,1,0:T(8,128)(2,1)S(1)}, bf16[512,16,128]{2,1,0:T(8,128)(2,1)}, u32[]{:S(2)}) copy-start(bf16[512,16,128]{2,1,0:T(8,128)(2,1)} %param.9) | copy-start | bytes 6291460
  36.8 2.6 %copy-start.8 = (bf16[512,16,128]{2,1,0:T(8,128)(2,1)S(1)}, bf16[512,16,128]{2,1,0:T(8,128)(2,1)}, u32[]{:S(2)}) copy-start(bf16[512,16,128]{2,1,0:T(8,128)(2,1)} %param.11) | copy-start | bytes 6291460
  38.0 1.3 copy-start.14
  117.3 5.3 %copy-start.5 = (bf16[512,16,128]{2,1,0:T(8,128)(2,1)S(1)}, bf16[512,16,128]{2,1,0:T(8,128)(2,1)}, u32[]{:S(2)}) copy-start(bf16[512,16,128]{2,1,0:T(8,128)(2,1)} %copy-done.3) | copy-start | bytes 6291460
  117.3 5.3 %copy-start.12 = (bf16[8,16,64,64]{3,2,1,0:T(8,128)(2,1)S(1)}, bf16[8,16,64,64]{3,2,1,0:T(8,128)(2,1)}, u32[]{:S(2)}) copy-start(bf16[8,16,64,64]{3,2,1,0:T(8,128)(2,1)} %select_convert_fusion) | copy-start | bytes 3145732
  126.6 54.5 %all-to-all-start.1 = ((bf16[512,16,128]{2,1,0:T(8,128)(2,1)}), bf16[512,16,128]{2,1,0:T(8,128)(2,1)}, u32[]{:S(2)}, u32[]{:S(2)}) async-start(bf16[512,16,128]{2,1,0:T(8,128)(2,1)} %bitcast.81), calls=%async_computation.1 | async-start | bytes 4194304 | tf_op jit(solution)/shard_map/all_to_all | solution.py:78
  181.1 30.3 %all-to-all-start.2 = ((bf16[512,16,128]{2,1,0:T(8,128)(2,1)}), bf16[512,16,128]{2,1,0:T(8,128)(2,1)}, u32[]{:S(2)}, u32[]{:S(2)}) async-start(bf16[512,16,128]{2,1,0:T(8,128)(2,1)} %bitcast.80), calls=%async_computation.2 | async-start | bytes 4194304 | tf_op jit(solution)/shard_map/all_to_all | solution.py:79
  185.8 7.1 %copy-start.9 = (bf16[512,16,128]{2,1,0:T(8,128)(2,1)S(1)}, bf16[512,16,128]{2,1,0:T(8,128)(2,1)}, u32[]{:S(2)}) copy-start(bf16[512,16,128]{2,1,0:T(8,128)(2,1)} %param.11) | copy-start | bytes 6291460
  192.9 3.0 %copy-start.1 = (bf16[8,16,128,128]{3,2,1,0:T(8,128)(2,1)}, bf16[8,16,128,128]{3,2,1,0:T(8,128)(2,1)S(1)}, u32[]{:S(2)}) copy-start(bf16[8,16,128,128]{3,2,1,0:T(8,128)(2,1)S(1)} %subtract_convert_fusion.1) | copy-start | bytes 12582916
  192.9 3.1 %copy-start.11 = (bf16[512,16,128]{2,1,0:T(8,128)(2,1)S(1)}, bf16[512,16,128]{2,1,0:T(8,128)(2,1)}, u32[]{:S(2)}) copy-start(bf16[512,16,128]{2,1,0:T(8,128)(2,1)} %param.9) | copy-start | bytes 6291460
  192.9 3.7 %copy-start.13 = (bf16[8,16,64,64]{3,2,1,0:T(8,128)(2,1)S(1)}, bf16[8,16,64,64]{3,2,1,0:T(8,128)(2,1)}, u32[]{:S(2)}) copy-start(bf16[8,16,64,64]{3,2,1,0:T(8,128)(2,1)} %select_convert_fusion) | copy-start | bytes 3145732
  211.4 30.2 %all-to-all-start = ((bf16[512,16,128]{2,1,0:T(8,128)(2,1)}), bf16[512,16,128]{2,1,0:T(8,128)(2,1)}, u32[]{:S(2)}, u32[]{:S(2)}) async-start(bf16[512,16,128]{2,1,0:T(8,128)(2,1)} %bitcast.82), calls=%async_computation | async-start | bytes 4194304 | tf_op jit(solution)/shard_map/all_to_all | solution.py:77
  215.8 2.8 %copy-start.2 = (bf16[8,16,128,128]{3,2,1,0:T(8,128)(2,1)S(1)}, bf16[8,16,128,128]{3,2,1,0:T(8,128)(2,1)}, u32[]{:S(2)}) copy-start(bf16[8,16,128,128]{3,2,1,0:T(8,128)(2,1)} %copy-done.1) | copy-start | bytes 12582916
  215.8 3.5 %copy-start.6 = (bf16[512,16,128]{2,1,0:T(8,128)(2,1)S(1)}, bf16[512,16,128]{2,1,0:T(8,128)(2,1)}, u32[]{:S(2)}) copy-start(bf16[512,16,128]{2,1,0:T(8,128)(2,1)} %copy-done.3) | copy-start | bytes 6291460
Sparse Core Ops, SparseCore 0:
  16.6 83.4 all-gather.6
  101.6 79.2 all-gather.4
where the time goes:
time: 253 us; the launch traced here: 252 us
  waiting for transfers between devices  113 us (45%)
  matrix products  40.3 us (16%)
  local copies, waits for them, and re-layouts  36.1 us (14%)
  other arithmetic  33.8 us (13%)
  between operations  14.3 us (6%)
  starting transfers between devices  13.7 us (5%)
    all_gather x2, waiting for transfers between devices, prefix(): gathered = lax.all_gather(part, axis)  91.3 us
    all_to_all x1, waiting for transfers between devices, per_device(): lax.all_to_all(query_grad, ('head', 'sub'), split_axis=0, concat_axis=1,...  11.1 us
    convert_element_type x1, other arithmetic, per_device(): suffix_low = suffix.astype(jnp.bfloat16)  11.1 us
    all_to_all x1, waiting for transfers between devices, per_device(): lax.all_to_all(value_grad, ('head', 'sub'), split_axis=0, concat_axis=1,...  11 us
    rev x1, local copies, waits for them, and re-layouts, per_device(): suffix = after[None] + jnp.cumsum(adj_block[::-1], 0)[::-1] - adj_block  8.35 us
    another operation x1, other arithmetic, per_device(): suffix = after[None] + jnp.cumsum(adj_block[::-1], 0)[::-1] - adj_block  8.32 us
    dot_general x1, matrix products, per_device(): jnp.einsum('nchd,nche->nhde', kch, vch, preferred_element_type=jnp.float32)  7.57 us
    another operation x1, other arithmetic, per_device(): state = before[None] + jnp.cumsum(kv_block, 0) - kv_block  7.04 us
  transfers between devices with their start and end apart: 5, of which 4 were waited for; matrix products, arithmetic and copies ran while one was open for 37% of the time, Pallas kernels for 0%

commit v1 on v0

--- a/solution.py
+++ b/solution.py
@@ -4,24 +4,22 @@
 from jax.sharding import PartitionSpec as P
 
 SPAN = 64
+PIECES = 4
+SEQ = 1
 
 
-def prefix(part, axis, combine, identity, reverse):
-    count = lax.axis_size(axis)
-    place = lax.axis_index(axis)
-    ahead = count - 1 - place if reverse else place
-    gathered = lax.all_gather(part, axis)
-    state = jnp.zeros_like(part) + jnp.asarray(identity, part.dtype)
-
-    def one(turn, state):
-        source = count - 1 - turn if reverse else turn
-        return combine(state, lax.dynamic_index_in_dim(gathered, source, 0, False))
-
-    return lax.fori_loop(0, ahead, one, state)
-
-
-def add_states(earlier, later):
-    return earlier + later
+def exclusive_scan(total, axis, count, reverse, pieces):
+    outs = []
+    for chunk in jnp.split(total, pieces, axis=0):
+        carried = jnp.zeros_like(chunk)
+        acc = jnp.zeros_like(chunk)
+        for hop in range(count - 1):
+            pair = (count - 1 - hop, count - 2 - hop) if reverse else (hop, hop + 1)
+            got = lax.ppermute(carried + chunk, axis, perm=[pair])
+            acc = acc + got
+            carried = got
+        outs.append(acc)
+    return jnp.concatenate(outs, 0)
 
 
 def per_device(queries, key_rows, value_rows, out_adjoint):
@@ -40,9 +38,8 @@
     adj_block = jnp.einsum("nche,nchd->nhed", dch, qsc, preferred_element_type=jnp.float32)
     kv_total = jnp.sum(kv_block, 0)
     adj_total = jnp.sum(adj_block, 0)
-    zeros = jnp.zeros_like(kv_total)
-    before = prefix(kv_total, "seq", add_states, zeros, False)
-    after = prefix(adj_total, "seq", add_states, zeros, True)
+    before = exclusive_scan(kv_total, "seq", SEQ, False, PIECES)
+    after = exclusive_scan(adj_total, "seq", SEQ, True, PIECES)
     state = before[None] + jnp.cumsum(kv_block, 0) - kv_block
     suffix = after[None] + jnp.cumsum(adj_block[::-1], 0)[::-1] - adj_block
     state_low = state.astype(jnp.bfloat16)
@@ -82,6 +79,8 @@
 
 
 def solution(mesh):
+    global SEQ
+    SEQ = mesh.shape["seq"]
     in_specs = (
         P(("grp", "seq"), ("head", "sub"), None),
         P(("grp", "seq"), ("head", "sub"), None),

time: 253 us -> 232 us (0.917)
  waiting for transfers between devices: 113 us -> 45.6 us
  starting transfers between devices: 13.7 us -> 70.5 us
  between operations: 14.3 us -> 1.3 us
  other arithmetic: 33.8 us -> 39.5 us
  local copies, waits for them, and re-layouts: 36.1 us -> 32.6 us
    all_gather x2 -> x0, waiting for transfers between devices: 91.3 us -> none  [prefix(): gathered = lax.all_gather(part, axis)]
    ppermute x0 -> x24, starting transfers between devices: none -> 56.8 us  [exclusive_scan(): got = lax.ppermute(carried + chunk, axis, perm=[pair])]
    ppermute x0 -> x24, waiting for transfers between devices: none -> 14.7 us  [exclusive_scan(): got = lax.ppermute(carried + chunk, axis, perm=[pair])]
    all_to_all x1, waiting for transfers between devices: 0.01 us -> 11 us  [per_device(): lax.all_to_all(key_grad, ('head', 'sub'), split_axis=0, concat_axis=1, ti...]
    add x3 -> x14, other arithmetic: 4.47 us -> 9.88 us  [the longest x8 5.2 us: exclusive_scan(): acc = acc + got]
    dot_general x1, matrix products: 4.3 us -> 1.23 us  [per_device(): jnp.einsum('nche,nshe->nhcs', dch, vch, preferred_element_type=jnp.float32)]
    dot_general x1, matrix products: 7.57 us -> 5.01 us  [per_device(): jnp.einsum('nchd,nche->nhde', kch, vch, preferred_element_type=jnp.float32)]
  transfers between devices with their start and end apart: 5 -> 27, of which waited for: 4 -> 7; matrix products, arithmetic and copies ran while one was open for 37% -> 43% of each run, Pallas kernels for 0% -> 0%
where the time goes in v1:
time: 232 us; the launch traced here: 231 us
  starting transfers between devices  70.5 us (30%)
  waiting for transfers between devices  45.6 us (20%)
  matrix products  41.8 us (18%)
  other arithmetic  39.5 us (17%)
  local copies, waits for them, and re-layouts  32.6 us (14%)
    ppermute x24, starting transfers between devices, exclusive_scan(): got = lax.ppermute(carried + chunk, axis, perm=[pair])  56.8 us
    ppermute x24, waiting for transfers between devices, exclusive_scan(): got = lax.ppermute(carried + chunk, axis, perm=[pair])  14.7 us
    all_to_all x1, waiting for transfers between devices, per_device(): lax.all_to_all(query_grad, ('head', 'sub'), split_axis=0, concat_axis=1,...  11.1 us
    all_to_all x1, waiting for transfers between devices, per_device(): lax.all_to_all(key_grad, ('head', 'sub'), split_axis=0, concat_axis=1, ti...  11 us
    convert_element_type x1, other arithmetic, per_device(): suffix_low = suffix.astype(jnp.bfloat16)  10.2 us
    all_to_all x1, waiting for transfers between devices, per_device(): lax.all_to_all(value_grad, ('head', 'sub'), split_axis=0, concat_axis=1,...  8.77 us
    another operation x1, other arithmetic, per_device(): suffix = after[None] + jnp.cumsum(adj_block[::-1], 0)[::-1] - adj_block  8.34 us
    rev x1, local copies, waits for them, and re-layouts, per_device(): suffix = after[None] + jnp.cumsum(adj_block[::-1], 0)[::-1] - adj_block  7.73 us
  transfers between devices with their start and end apart: 27, of which 7 were waited for; matrix products, arithmetic and copies ran while one was open for 43% of the time, Pallas kernels for 0%

profile of v1, /device:TPU:0, one launch (start us, length us, event | category | flops | bytes accessed | tf_op | source)
XLA Modules:
  0.0 231.3 jit_solution(3426260815916196891)
XLA Ops:
  3.6 5.0 %fusion.27 = (f32[16,128,128]{1,2,0:T(8,128)S(1)}, f32[8,16,128,128]{2,3,1,0:T(8,128)}) fusion(bf16[8,64,16,128]{3,2,1,0:T(8,128)(2,1)S(1)} %bitcast.66, bf16[8,64,16,128]{3,2,1,0:T(8,128)(2,1)S(1)} %bitcast.58), kind=kOutput, calls=%fused_computation.66 | convolution fusion | flops 270270464 | bytes 13631488 | tf_op jit(solution)/shard_map/nche,nchd->nhed/dot_general | solution.py:38
  10.8 5.0 %fusion.26 = (f32[16,128,128]{2,1,0:T(8,128)S(1)}, f32[8,16,128,128]{3,2,1,0:T(8,128)}) fusion(bf16[8,64,16,128]{3,2,1,0:T(8,128)(2,1)S(1)} %bitcast.54, bf16[8,64,16,128]{3,2,1,0:T(8,128)(2,1)S(1)} %bitcast.64), kind=kOutput, calls=%fused_computation.65 | convolution fusion | flops 270270464 | bytes 13631488 | tf_op jit(solution)/shard_map/nchd,nche->nhde/dot_general | solution.py:37
  16.5 4.9 %collective-permute-start = (f32[4,128,128]{2,1,0:T(8,128)}, f32[4,128,128]{2,1,0:T(8,128)S(1)}, u32[]{:S(2)}, u32[]{:S(2)}) collective-permute-start(f32[4,128,128]{2,1,0:T(8,128)} %split.32), channel_id=1, source_target_pairs={{0,4},{1,5},{2,6},{3,7},{16,20},{17,21},{18,22},{19,23}} | collective-permute-start | bytes 786440 | tf_op jit(solution)/shard_map/ppermute | solution.py:18
  28.3 7.7 %rev.6 = f32[8,16,128,128]{2,3,1,0:T(8,128)} reverse(f32[8,16,128,128]{2,3,1,0:T(8,128)} %get-tuple-element.29), dimensions={0} | reverse | bytes 16777216 | tf_op jit(solution)/shard_map/rev | solution.py:44
  36.1 8.3 %fusion.28 = f32[8,16,128,128]{2,3,1,0:T(8,128)} fusion(f32[8,16,128,128]{2,3,1,0:T(8,128)} %rev.6), kind=kOutput, calls=%fused_computation.67 | output fusion | flops 14680064 | bytes 16777216 | tf_op jit(solution)/shard_map/jit(cumsum)/reduce_window_sum | solution.py:44
  44.4 3.5 %select_convert_fusion.1 = bf16[8,16,64,64]{3,2,1,0:T(8,128)(2,1)S(1)} fusion(pred[64,64]{1,0:T(8,128)(4,1)S(1)} %iota_compare_fusion, bf16[8,64,16,128]{3,2,1,0:T(8,128)(2,1)} %bitcast.60, bf16[8,64,16,128]{3,2,1,0:T(8,128)(2,1)} %bitcast.62), kind=kOutput, calls=%fused_computation.11 | convolution fusion | flops 135266304 | bytes 5246976 | tf_op jit(solution)/shard_map/nchd,nshd->nhcs/dot_general | solution.py:50
  58.5 23.5 %collective-permute-start.3 = (f32[4,128,128]{2,1,0:T(8,128)S(1)}, f32[4,128,128]{2,1,0:T(8,128)S(1)}, u32[]{:S(2)}, u32[]{:S(2)}) collective-permute-start(f32[4,128,128]{2,1,0:T(8,128)S(1)} %get-tuple-element.22), channel_id=1, source_target_pairs={{0,4},{1,5},{2,6},{3,7},{16,20},{17,21},{18,22},{19,23}} | collective-permute-start | bytes 786440 | tf_op jit(solution)/shard_map/ppermute | solution.py:18
  84.3 5.6 %collective-permute-start.9 = (f32[4,128,128]{2,1,0:T(8,128)S(1)}, f32[4,128,128]{2,1,0:T(8,128)S(1)}, u32[]{:S(2)}, u32[]{:S(2)}) collective-permute-start(f32[4,128,128]{2,1,0:T(8,128)S(1)} %get-tuple-element.20), channel_id=1, source_target_pairs={{0,4},{1,5},{2,6},{3,7},{16,20},{17,21},{18,22},{19,23}} | collective-permute-start | bytes 786440 | tf_op jit(solution)/shard_map/ppermute | solution.py:18
  94.3 2.9 %collective-permute-done.9 = f32[4,128,128]{2,1,0:T(8,128)S(1)} collective-permute-done((f32[4,128,128]{2,1,0:T(8,128)S(1)}, f32[4,128,128]{2,1,0:T(8,128)S(1)}, u32[]{:S(2)}, u32[]{:S(2)}) %collective-permute-start.9) | collective-permute-done | bytes 262176 | tf_op jit(solution)/shard_map/ppermute | solution.py:18
  106.1 8.7 %collective-permute-done.20 = f32[4,128,128]{1,2,0:T(8,128)S(1)} collective-permute-done((f32[4,128,128]{1,2,0:T(8,128)S(1)}, f32[4,128,128]{1,2,0:T(8,128)S(1)}, u32[]{:S(2)}, u32[]{:S(2)}) %collective-permute-start.20) | collective-permute-done | bytes 262176 | tf_op jit(solution)/shard_map/ppermute | solution.py:18
  118.7 10.2 %subtract_convert_fusion = bf16[8,16,128,128]{2,3,1,0:T(8,128)(2,1)} fusion(f32[8,16,128,128]{2,3,1,0:T(8,128)} %get-tuple-element.29, f32[8,16,128,128]{2,3,1,0:T(8,128)} %fusion.28, f32[16,128,128]{1,2,0:T(8,128)} %pad_maximum_fusion.1), kind=kLoop, calls=%fused_computation | loop fusion | flops 6291456 | bytes 22020096 | tf_op jit(solution)/shard_map/convert_element_type | solution.py:46
  128.9 5.3 %fusion = bf16[8,64,16,128]{3,1,2,0:T(8,128)(2,1)S(1)} fusion(f32[8,16,64,128]{3,2,1,0:T(8,128)} %fusion.5, bf16[8,16,128,128]{2,3,1,0:T(8,128)(2,1)} %subtract_convert_fusion, bf16[8,64,16,128]{3,2,1,0:T(8,128)(2,1)} %bitcast.63), kind=kOutput, calls=%fused_computation.3 | convolution fusion | flops 270532608 | bytes 12582912 | tf_op jit(solution)/shard_map/nshd,nhed->nshe/dot_general | solution.py:65
  136.9 4.5 %all-to-all-start.2 = ((bf16[512,16,128]{2,1,0:T(8,128)(2,1)}), bf16[512,16,128]{2,1,0:T(8,128)(2,1)}, u32[]{:S(2)}, u32[]{:S(2)}) async-start(bf16[512,16,128]{2,1,0:T(8,128)(2,1)} %bitcast.70), calls=%async_computation.2 | async-start | bytes 4194304 | tf_op jit(solution)/shard_map/all_to_all | solution.py:76
  147.1 6.5 %fusion.4 = bf16[8,64,16,128]{3,1,2,0:T(8,128)(2,1)S(1)} fusion(f32[8,16,128,64]{2,3,1,0:T(8,128)} %fusion.10, bf16[8,16,128,128]{2,3,1,0:T(8,128)(2,1)} %subtract_convert_fusion, bf16[8,64,16,128]{3,2,1,0:T(8,128)(2,1)S(1)} %bitcast.55), kind=kOutput, calls=%fused_computation.14 | convolution fusion | flops 270532608 | bytes 12582912 | tf_op jit(solution)/shard_map/nshe,nhed->nshd/dot_general | solution.py:62
  158.4 8.8 %all-to-all-done.2 = bf16[512,16,128]{2,1,0:T(8,128)(2,1)} async-done(((bf16[512,16,128]{2,1,0:T(8,128)(2,1)}), bf16[512,16,128]{2,1,0:T(8,128)(2,1)}, u32[]{:S(2)}, u32[]{:S(2)}) %all-to-all-start.2) | async-done | bytes 2097184 | tf_op jit(solution)/shard_map/all_to_all | solution.py:76
  167.2 4.8 %all-to-all-start.1 = ((bf16[512,16,128]{2,1,0:T(8,128)(2,1)}), bf16[512,16,128]{2,1,0:T(8,128)(2,1)}, u32[]{:S(2)}, u32[]{:S(2)}) async-start(bf16[512,16,128]{2,1,0:T(8,128)(2,1)} %bitcast.71), calls=%async_computation.1 | async-start | bytes 4194304 | tf_op jit(solution)/shard_map/all_to_all | solution.py:75
  173.2 7.1 %subtract_convert_fusion.1 = bf16[8,16,128,128]{3,2,1,0:T(8,128)(2,1)S(1)} fusion(f32[8,16,128,128]{3,2,1,0:T(8,128)} %get-tuple-element.27, f32[16,128,128]{2,1,0:T(8,128)S(1)} %pad_maximum_fusion), kind=kOutput, calls=%fused_computation.1 | output fusion | flops 20971520 | bytes 13631488 | tf_op jit(solution)/shard_map/jit(cumsum)/reduce_window_sum | solution.py:43
  180.8 3.0 %fusion.2 = bf16[8,64,16,128]{3,1,2,0:T(8,128)(2,1)S(1)} fusion(f32[8,16,64,128]{3,2,1,0:T(8,128)S(1)} %copy-done.9, bf16[8,16,128,128]{3,2,1,0:T(8,128)(2,1)S(1)} %subtract_convert_fusion.1, f32[8,64]{1,0:T(8,128)S(1)} %multiply_rsqrt_fusion, bf16[8,64,16,128]{3,2,1,0:T(8,128)(2,1)S(1)} %bitcast.69), kind=kOutput, calls=%fused_computation.6 | convolution fusion | flops 271581184 | bytes 12584960 | tf_op jit(solution)/shard_map/nche,nhde->nchd/dot_general | solution.py:59
  186.6 11.0 %all-to-all-done.1 = bf16[512,16,128]{2,1,0:T(8,128)(2,1)} async-done(((bf16[512,16,128]{2,1,0:T(8,128)(2,1)}), bf16[512,16,128]{2,1,0:T(8,128)(2,1)}, u32[]{:S(2)}, u32[]{:S(2)}) %all-to-all-start.1) | async-done | bytes 2097184 | tf_op jit(solution)/shard_map/all_to_all | solution.py:75
  197.5 4.5 %all-to-all-start = ((bf16[512,16,128]{2,1,0:T(8,128)(2,1)}), bf16[512,16,128]{2,1,0:T(8,128)(2,1)}, u32[]{:S(2)}, u32[]{:S(2)}) async-start(bf16[512,16,128]{2,1,0:T(8,128)(2,1)} %bitcast.72), calls=%async_computation | async-start | bytes 4194304 | tf_op jit(solution)/shard_map/all_to_all | solution.py:74
  209.5 3.6 %copy.78 = bf16[128,4,16,128]{3,2,1,0:T(8,128)(2,1)} copy(bf16[128,4,16,128]{3,2,0,1:T(8,128)(2,1)} %bitcast.23) | data formatting | bytes 4194304 | tf_op jit(solution)/shard_map/all_to_all | solution.py:76
  213.0 3.6 %copy.72 = bf16[128,4,16,128]{3,2,1,0:T(8,128)(2,1)} copy(bf16[128,4,16,128]{3,2,0,1:T(8,128)(2,1)} %bitcast.17) | data formatting | bytes 4194304 | tf_op jit(solution)/shard_map/all_to_all | solution.py:75
  216.6 11.1 %all-to-all-done = bf16[512,16,128]{2,1,0:T(8,128)(2,1)} async-done(((bf16[512,16,128]{2,1,0:T(8,128)(2,1)}), bf16[512,16,128]{2,1,0:T(8,128)(2,1)}, u32[]{:S(2)}, u32[]{:S(2)}) %all-to-all-start) | async-done | bytes 2097184 | tf_op jit(solution)/shard_map/all_to_all | solution.py:74
  227.7 3.6 %copy.64 = bf16[128,4,16,128]{3,2,1,0:T(8,128)(2,1)} copy(bf16[128,4,16,128]{3,2,0,1:T(8,128)(2,1)} %bitcast.11) | data formatting | bytes 4194304 | tf_op jit(solution)/shard_map/all_to_all | solution.py:74
  (117 shorter events, 67.4 us)
Async XLA Ops:
  9.4 38.6 %collective-permute-start.12 = (f32[4,128,128]{1,2,0:T(8,128)}, f32[4,128,128]{1,2,0:T(8,128)}, u32[]{:S(2)}, u32[]{:S(2)}) collective-permute-start(f32[4,128,128]{1,2,0:T(8,128)} %split.36), channel_id=1, source_target_pairs={{12,8},{13,9},{14,10},{15,11},{28,24},{29,25},{30,26},{31,27}} | collective-permute-start | bytes 786440 | tf_op jit(solution)/shard_map/ppermute | solution.py:18
  16.5 41.2 %collective-permute-start = (f32[4,128,128]{2,1,0:T(8,128)}, f32[4,128,128]{2,1,0:T(8,128)S(1)}, u32[]{:S(2)}, u32[]{:S(2)}) collective-permute-start(f32[4,128,128]{2,1,0:T(8,128)} %split.32), channel_id=1, source_target_pairs={{0,4},{1,5},{2,6},{3,7},{16,20},{17,21},{18,22},{19,23}} | collective-permute-start | bytes 786440 | tf_op jit(solution)/shard_map/ppermute | solution.py:18
  49.4 5.8 %collective-permute-start.13 = (f32[4,128,128]{1,2,0:T(8,128)S(1)}, f32[4,128,128]{1,2,0:T(8,128)S(1)}, u32[]{:S(2)}, u32[]{:S(2)}) collective-permute-start(f32[4,128,128]{1,2,0:T(8,128)S(1)} %get-tuple-element.8), channel_id=1, source_target_pairs={{8,4},{9,5},{10,6},{11,7},{24,20},{25,21},{26,22},{27,23}} | collective-permute-start | bytes 786440 | tf_op jit(solution)/shard_map/ppermute | solution.py:18
  55.4 26.6 %collective-permute-start.16 = (f32[4,128,128]{1,2,0:T(8,128)S(1)}, f32[4,128,128]{1,2,0:T(8,128)S(1)}, u32[]{:S(2)}, u32[]{:S(2)}) collective-permute-start(f32[4,128,128]{1,2,0:T(8,128)S(1)} %get-tuple-element.5), channel_id=1, source_target_pairs={{8,4},{9,5},{10,6},{11,7},{24,20},{25,21},{26,22},{27,23}} | collective-permute-start | bytes 786440 | tf_op jit(solution)/shard_map/ppermute | solution.py:18
  56.3 28.0 %collective-permute-start.19 = (f32[4,128,128]{1,2,0:T(8,128)S(1)}, f32[4,128,128]{1,2,0:T(8,128)S(1)}, u32[]{:S(2)}, u32[]{:S(2)}) collective-permute-start(f32[4,128,128]{1,2,0:T(8,128)S(1)} %get-tuple-element.6), channel_id=1, source_target_pairs={{8,4},{9,5},{10,6},{11,7},{24,20},{25,21},{26,22},{27,23}} | collective-permute-start | bytes 786440 | tf_op jit(solution)/shard_map/ppermute | solution.py:18
  57.0 33.0 %collective-permute-start.22 = (f32[4,128,128]{1,2,0:T(8,128)S(1)}, f32[4,128,128]{1,2,0:T(8,128)S(1)}, u32[]{:S(2)}, u32[]{:S(2)}) collective-permute-start(f32[4,128,128]{1,2,0:T(8,128)S(1)} %get-tuple-element.7), channel_id=1, source_target_pairs={{8,4},{9,5},{10,6},{11,7},{24,20},{25,21},{26,22},{27,23}} | collective-permute-start | bytes 786440 | tf_op jit(solution)/shard_map/ppermute | solution.py:18
  57.8 33.6 %collective-permute-start.1 = (f32[4,128,128]{2,1,0:T(8,128)S(1)}, f32[4,128,128]{2,1,0:T(8,128)S(1)}, u32[]{:S(2)}, u32[]{:S(2)}) collective-permute-start(f32[4,128,128]{2,1,0:T(8,128)S(1)} %get-tuple-element.19), channel_id=1, source_target_pairs={{4,8},{5,9},{6,10},{7,11},{20,24},{21,25},{22,26},{23,27}} | collective-permute-start | bytes 786440 | tf_op jit(solution)/shard_map/ppermute | solution.py:18
  58.5 34.2 %collective-permute-start.3 = (f32[4,128,128]{2,1,0:T(8,128)S(1)}, f32[4,128,128]{2,1,0:T(8,128)S(1)}, u32[]{:S(2)}, u32[]{:S(2)}) collective-permute-start(f32[4,128,128]{2,1,0:T(8,128)S(1)} %get-tuple-element.22), channel_id=1, source_target_pairs={{0,4},{1,5},{2,6},{3,7},{16,20},{17,21},{18,22},{19,23}} | collective-permute-start | bytes 786440 | tf_op jit(solution)/shard_map/ppermute | solution.py:18
  82.0 12.3 %collective-permute-start.6 = (f32[4,128,128]{2,1,0:T(8,128)S(1)}, f32[4,128,128]{2,1,0:T(8,128)S(1)}, u32[]{:S(2)}, u32[]{:S(2)}) collective-permute-start(f32[4,128,128]{2,1,0:T(8,128)S(1)} %get-tuple-element.21), channel_id=1, source_target_pairs={{0,4},{1,5},{2,6},{3,7},{16,20},{17,21},{18,22},{19,23}} | collective-permute-start | bytes 786440 | tf_op jit(solution)/shard_map/ppermute | solution.py:18
  84.3 13.0 %collective-permute-start.9 = (f32[4,128,128]{2,1,0:T(8,128)S(1)}, f32[4,128,128]{2,1,0:T(8,128)S(1)}, u32[]{:S(2)}, u32[]{:S(2)}) collective-permute-start(f32[4,128,128]{2,1,0:T(8,128)S(1)} %get-tuple-element.20), channel_id=1, source_target_pairs={{0,4},{1,5},{2,6},{3,7},{16,20},{17,21},{18,22},{19,23}} | collective-permute-start | bytes 786440 | tf_op jit(solution)/shard_map/ppermute | solution.py:18
  90.0 12.5 %collective-permute-start.14 = (f32[4,128,128]{1,2,0:T(8,128)S(1)}, f32[4,128,128]{1,2,0:T(8,128)S(1)}, u32[]{:S(2)}, u32[]{:S(2)}) collective-permute-start(f32[4,128,128]{1,2,0:T(8,128)S(1)} %get-tuple-element.4), channel_id=1, source_target_pairs={{4,0},{5,1},{6,2},{7,3},{20,16},{21,17},{22,18},{23,19}} | collective-permute-start | bytes 786440 | tf_op jit(solution)/shard_map/ppermute | solution.py:18
  91.4 13.4 %collective-permute-start.17 = (f32[4,128,128]{1,2,0:T(8,128)S(1)}, f32[4,128,128]{1,2,0:T(8,128)S(1)}, u32[]{:S(2)}, u32[]{:S(2)}) collective-permute-start(f32[4,128,128]{1,2,0:T(8,128)S(1)} %get-tuple-element.12), channel_id=1, source_target_pairs={{4,0},{5,1},{6,2},{7,3},{20,16},{21,17},{22,18},{23,19}} | collective-permute-start | bytes 786440 | tf_op jit(solution)/shard_map/ppermute | solution.py:18
  98.3 43.1 %collective-permute-start.10 = (f32[4,128,128]{2,1,0:T(8,128)}, f32[4,128,128]{2,1,0:T(8,128)}, u32[]{:S(2)}, u32[]{:S(2)}) collective-permute-start(f32[4,128,128]{2,1,0:T(8,128)} %get-tuple-element.18), channel_id=1, source_target_pairs={{4,8},{5,9},{6,10},{7,11},{20,24},{21,25},{22,26},{23,27}} | collective-permute-start | bytes 786440 | tf_op jit(solution)/shard_map/ppermute | solution.py:18
  99.7 41.7 %collective-permute-start.4 = (f32[4,128,128]{2,1,0:T(8,128)}, f32[4,128,128]{2,1,0:T(8,128)}, u32[]{:S(2)}, u32[]{:S(2)}) collective-permute-start(f32[4,128,128]{2,1,0:T(8,128)} %get-tuple-element.16), channel_id=1, source_target_pairs={{4,8},{5,9},{6,10},{7,11},{20,24},{21,25},{22,26},{23,27}} | collective-permute-start | bytes 786440 | tf_op jit(solution)/shard_map/ppermute | solution.py:18
  101.0 40.4 %collective-permute-start.7 = (f32[4,128,128]{2,1,0:T(8,128)}, f32[4,128,128]{2,1,0:T(8,128)}, u32[]{:S(2)}, u32[]{:S(2)}) collective-permute-start(f32[4,128,128]{2,1,0:T(8,128)} %get-tuple-element.17), channel_id=1, source_target_pairs={{4,8},{5,9},{6,10},{7,11},{20,24},{21,25},{22,26},{23,27}} | collective-permute-start | bytes 786440 | tf_op jit(solution)/shard_map/ppermute | solution.py:18
  102.4 12.4 %collective-permute-start.20 = (f32[4,128,128]{1,2,0:T(8,128)S(1)}, f32[4,128,128]{1,2,0:T(8,128)S(1)}, u32[]{:S(2)}, u32[]{:S(2)}) collective-permute-start(f32[4,128,128]{1,2,0:T(8,128)S(1)} %get-tuple-element.13), channel_id=1, source_target_pairs={{4,0},{5,1},{6,2},{7,3},{20,16},{21,17},{22,18},{23,19}} | collective-permute-start | bytes 786440 | tf_op jit(solution)/shard_map/ppermute | solution.py:18
  104.7 12.8 %collective-permute-start.23 = (f32[4,128,128]{1,2,0:T(8,128)S(1)}, f32[4,128,128]{1,2,0:T(8,128)S(1)}, u32[]{:S(2)}, u32[]{:S(2)}) collective-permute-start(f32[4,128,128]{1,2,0:T(8,128)S(1)} %get-tuple-element.14), channel_id=1, source_target_pairs={{4,0},{5,1},{6,2},{7,3},{20,16},{21,17},{22,18},{23,19}} | collective-permute-start | bytes 786440 | tf_op jit(solution)/shard_map/ppermute | solution.py:18
  114.8 31.3 %collective-permute-start.2 = (f32[4,128,128]{2,1,0:T(8,128)}, f32[4,128,128]{2,1,0:T(8,128)}, u32[]{:S(2)}, u32[]{:S(2)}) collective-permute-start(f32[4,128,128]{2,1,0:T(8,128)} %get-tuple-element.15), channel_id=1, source_target_pairs={{8,12},{9,13},{10,14},{11,15},{24,28},{25,29},{26,30},{27,31}} | collective-permute-start | bytes 786440 | tf_op jit(solution)/shard_map/ppermute | solution.py:18
  136.9 30.2 %all-to-all-start.2 = ((bf16[512,16,128]{2,1,0:T(8,128)(2,1)}), bf16[512,16,128]{2,1,0:T(8,128)(2,1)}, u32[]{:S(2)}, u32[]{:S(2)}) async-start(bf16[512,16,128]{2,1,0:T(8,128)(2,1)} %bitcast.70), calls=%async_computation.2 | async-start | bytes 4194304 | tf_op jit(solution)/shard_map/all_to_all | solution.py:76
  143.4 10.2 %collective-permute-start.5 = (f32[4,128,128]{2,1,0:T(8,128)S(1)}, f32[4,128,128]{2,1,0:T(8,128)S(1)}, u32[]{:S(2)}, u32[]{:S(2)}) collective-permute-start(f32[4,128,128]{2,1,0:T(8,128)S(1)} %get-tuple-element.23), channel_id=1, source_target_pairs={{8,12},{9,13},{10,14},{11,15},{24,28},{25,29},{26,30},{27,31}} | collective-permute-start | bytes 786440 | tf_op jit(solution)/shard_map/ppermute | solution.py:18
  144.0 13.3 %collective-permute-start.8 = (f32[4,128,128]{2,1,0:T(8,128)S(1)}, f32[4,128,128]{2,1,0:T(8,128)S(1)}, u32[]{:S(2)}, u32[]{:S(2)}) collective-permute-start(f32[4,128,128]{2,1,0:T(8,128)S(1)} %get-tuple-element.24), channel_id=1, source_target_pairs={{8,12},{9,13},{10,14},{11,15},{24,28},{25,29},{26,30},{27,31}} | collective-permute-start | bytes 786440 | tf_op jit(solution)/shard_map/ppermute | solution.py:18
  144.7 27.3 %collective-permute-start.11 = (f32[4,128,128]{2,1,0:T(8,128)}, f32[4,128,128]{2,1,0:T(8,128)}, u32[]{:S(2)}, u32[]{:S(2)}) collective-permute-start(f32[4,128,128]{2,1,0:T(8,128)} %get-tuple-element.25), channel_id=1, source_target_pairs={{8,12},{9,13},{10,14},{11,15},{24,28},{25,29},{26,30},{27,31}} | collective-permute-start | bytes 786440 | tf_op jit(solution)/shard_map/ppermute | solution.py:18
  167.2 30.4 %all-to-all-start.1 = ((bf16[512,16,128]{2,1,0:T(8,128)(2,1)}), bf16[512,16,128]{2,1,0:T(8,128)(2,1)}, u32[]{:S(2)}, u32[]{:S(2)}) async-start(bf16[512,16,128]{2,1,0:T(8,128)(2,1)} %bitcast.71), calls=%async_computation.1 | async-start | bytes 4194304 | tf_op jit(solution)/shard_map/all_to_all | solution.py:75
  197.5 30.2 %all-to-all-start = ((bf16[512,16,128]{2,1,0:T(8,128)(2,1)}), bf16[512,16,128]{2,1,0:T(8,128)(2,1)}, u32[]{:S(2)}, u32[]{:S(2)}) async-start(bf16[512,16,128]{2,1,0:T(8,128)(2,1)} %bitcast.72), calls=%async_computation | async-start | bytes 4194304 | tf_op jit(solution)/shard_map/all_to_all | solution.py:74
  (24 other events, 160.7 us)
